TPU v7x, 128 devices: a whole 4x4x4 slice. The times are simulated.
128 devices in a mesh: req: 16 (over y, x), kv: 8 (over z, core).
Axes of the slice: x: 4, y: 4, z: 4, core: 2. Of those that a mesh axis runs over, the one named last changes fastest.
Arguments:
- hidden: bfloat16 [1024, 1536], P('req', 'kv'), may hold values from -6 to 6
- perm: int32 [1024], replicated, may hold values from 0 to 1023, as said below
- seq_lens: int32 [1024], P('req'), may hold values from 1 to 4096, as said below
- page_table: int32 [1024, 32], P('req'), may hold values from 0 to 319, as said below
- kv_cache: bfloat16 [5120, 8, 128, 128], P('req', 'kv'), may hold values from -52 to 52
- attn_gain: float32 [1536], replicated, may hold values from 0.1 to 1.9
- qkv_weight: bfloat16 [8, 1536, 320], P('kv'), may hold values from -0.15625 to 0.15625
- out_weight: bfloat16 [8, 192, 1536], P('kv'), may hold values from -1 to 1
- ffn_gain: float32 [1536], replicated, may hold values from 0.1 to 1.9
- router: bfloat16 [1536, 16], replicated, may hold values from -0.15625 to 0.15625
- routes: int32 [1024, 2], P(('req', 'kv')), may hold values from 0 to 15, all different within a row; in each aligned block of 8 rows (0 to 7, 8 to 15, ...) at most 2 rows name the same one
- gate_up: bfloat16 [16, 1536, 2048], P('req'), may hold values from -0.15625 to 0.15625
- down: bfloat16 [16, 1024, 1536], P('req'), may hold values from -0.1875 to 0.1875
Outputs:
- mixed: bfloat16 [1024, 1536], P(('req', 'kv'))
Inputs may be any that keep to these rules, and one draw needn't show every extreme that they name: A permutation of the 1024 requests: slot s holds request perm[s]. The 64 slots of each index of req hold exactly 4 requests from each block of 64 consecutive requests. `seq_lens`: the length 4096 is reached on every index of req. `page_table`: entries 0 to (seq_lens[s] + 127) // 128 - 1 of row s are used; no page of one index of req is used by two of its slots; later entries name arbitrary pages.
All inputs are finite; a program needn't handle non-finite values.
Results may differ from a plain program's by a relative error of at most 0.017.
Values may be sent and summed in bfloat16 or wider, within the bound.
No kernel may reach another device: no remote copies, remote signals or barrier semaphores. Data moves between devices by JAX's collectives and lax.ppermute only.
A program may use at most 128 MiB of HBM per device.

v0:
```python
import jax
import jax.numpy as jnp
from jax import lax
from jax.sharding import PartitionSpec as P

REQ_DEV = 64
NEG_FILL = -1e30
EPS_NORM = 1e-05


def rms_norm(values, gain_vec):
    values = values.astype(jnp.float32)
    factor = lax.rsqrt(jnp.mean(values * values, axis=-1, keepdims=True) + EPS_NORM)
    return (values * factor * gain_vec).astype(jnp.bfloat16)


def attend(normed, seq_lens, page_table, kv_cache, qkv_weight):
    pool_pages, local_heads, twice_hd, page_len = kv_cache.shape
    head_dim = twice_hd // 2
    slot_count = normed.shape[0]
    groups = qkv_weight.shape[2] // head_dim - 2
    max_pages = page_table.shape[1]
    projected = jnp.einsum("sd,hdc->shc", normed, qkv_weight, preferred_element_type=jnp.float32)
    queries = (
        projected[:, :, : groups * head_dim]
        .reshape(slot_count, local_heads, groups, head_dim)
        .astype(jnp.bfloat16)
    )
    key_new = projected[:, :, groups * head_dim : (groups + 1) * head_dim].astype(jnp.bfloat16)
    value_new = projected[:, :, (groups + 1) * head_dim :].astype(jnp.bfloat16)
    page_need = (seq_lens + page_len - 1) // page_len
    page_ids = jnp.arange(max_pages, dtype=jnp.int32)
    in_use = page_ids[None, :] < page_need[:, None]
    target_page = jnp.where(in_use, page_table, pool_pages).reshape(-1)
    slot_ids = jnp.broadcast_to(
        jnp.arange(slot_count, dtype=jnp.int32)[:, None], (slot_count, max_pages)
    ).reshape(-1)
    order_ids = jnp.broadcast_to(page_ids[None, :], (slot_count, max_pages)).reshape(-1)
    owner = (
        jnp.full((pool_pages,), slot_count, jnp.int32).at[target_page].set(slot_ids, mode="drop")
    )
    page_order = jnp.zeros((pool_pages,), jnp.int32).at[target_page].set(order_ids, mode="drop")
    owner_safe = jnp.minimum(owner, slot_count - 1)
    position = page_order[:, None] * page_len + jnp.arange(page_len, dtype=jnp.int32)[None, :]
    live = (owner[:, None] < slot_count) & (position < jnp.take(seq_lens, owner_safe)[:, None])
    scale_factor = head_dim ** (-0.5)
    page_queries = jnp.take(queries, owner_safe, axis=0)
    scores = (
        jnp.einsum(
            "pkgd,pkdt->pkgt",
            page_queries,
            kv_cache[:, :, :head_dim, :],
            preferred_element_type=jnp.float32,
        )
        * scale_factor
    )
    scores = jnp.where(live[:, None, None, :], scores, NEG_FILL)
    score_new = (
        jnp.einsum("skgd,skd->skg", queries, key_new, preferred_element_type=jnp.float32)
        * scale_factor
    )
    page_peak = jnp.max(scores, axis=3)
    belongs = owner[None, :] == jnp.arange(slot_count, dtype=jnp.int32)[:, None]
    slot_peak = jnp.max(jnp.where(belongs[:, :, None, None], page_peak[None], NEG_FILL), axis=1)
    slot_peak = jnp.maximum(slot_peak, score_new)
    weights = jnp.where(
        live[:, None, None, :],
        jnp.exp(scores - jnp.take(slot_peak, owner_safe, axis=0)[..., None]),
        0.0,
    )
    page_total = jnp.sum(weights, axis=3)
    page_value = jnp.einsum(
        "pkgt,pkdt->pkgd",
        weights.astype(jnp.bfloat16),
        kv_cache[:, :, head_dim:, :],
        preferred_element_type=jnp.float32,
    )
    belongs_f = belongs.astype(jnp.float32)
    total_sum = jnp.dot(
        belongs_f, page_total.reshape(pool_pages, -1), precision=lax.Precision.HIGHEST
    ).reshape(slot_count, local_heads, groups)
    value_sum = jnp.dot(
        belongs_f, page_value.reshape(pool_pages, -1), precision=lax.Precision.HIGHEST
    ).reshape(slot_count, local_heads, groups, head_dim)
    weight_new = jnp.exp(score_new - slot_peak)
    total_sum = total_sum + weight_new
    rounded_new = lax.optimization_barrier(weight_new.astype(jnp.bfloat16)).astype(jnp.float32)
    value_sum = value_sum + rounded_new[..., None] * value_new.astype(jnp.float32)[:, :, None, :]
    return (value_sum / total_sum[..., None]).astype(jnp.bfloat16).reshape(slot_count, -1)


def expert_apply(piece, gate_up, down):
    n_source, slot_num, local_experts, width = piece.shape
    rows_in = piece.transpose(2, 0, 1, 3).reshape(local_experts, n_source * slot_num, width)
    projected_up = jnp.einsum("erd,edf->erf", rows_in, gate_up, preferred_element_type=jnp.float32)
    hidden_units = gate_up.shape[2] // 2
    acts = (
        jax.nn.silu(projected_up[..., :hidden_units]) * projected_up[..., hidden_units:]
    ).astype(jnp.bfloat16)
    result = jnp.einsum("erf,efd->erd", acts, down, preferred_element_type=jnp.float32).astype(
        jnp.bfloat16
    )
    return result.reshape(local_experts, n_source, slot_num, width).transpose(1, 2, 0, 3)


def shards(
    hidden,
    perm,
    seq_lens,
    page_table,
    kv_cache,
    attn_gain,
    qkv_weight,
    out_weight,
    ffn_gain,
    router,
    routes,
    gate_up,
    down,
):
    req_index = lax.axis_index("req")
    kv_index = lax.axis_index("kv")
    every_row = lax.all_gather(hidden, "req", axis=0, tiled=True)
    my_perm = lax.dynamic_slice_in_dim(perm, req_index * REQ_DEV, REQ_DEV)
    picked_rows = jnp.take(every_row, my_perm, axis=0)
    tokens = lax.all_gather(picked_rows, "kv", axis=1, tiled=True)
    normed = rms_norm(tokens, attn_gain)
    head_out = attend(normed, seq_lens, page_table, kv_cache, qkv_weight)
    sub_rows = routes.shape[0]
    width = tokens.shape[1]
    out_flat = out_weight.reshape(-1, out_weight.shape[2])
    attn_rows = lax.psum_scatter(
        jnp.dot(head_out, out_flat, preferred_element_type=jnp.float32).astype(jnp.bfloat16),
        "kv",
        scatter_dimension=0,
        tiled=True,
    ).astype(jnp.float32)
    own_tokens = lax.dynamic_slice_in_dim(tokens, kv_index * sub_rows, sub_rows, 0)
    residual = (own_tokens.astype(jnp.float32) + attn_rows).astype(jnp.bfloat16)
    normed_ffn = rms_norm(residual, ffn_gain)
    logits = jnp.dot(normed_ffn, router, preferred_element_type=jnp.float32)
    chosen = jnp.take_along_axis(logits, routes, axis=1)
    sigmoid_vals = jax.nn.sigmoid(chosen)
    gates = sigmoid_vals / jnp.sum(sigmoid_vals, axis=1, keepdims=True)
    experts_all = router.shape[1]
    n_req = lax.axis_size("req")
    local_experts = gate_up.shape[0]
    capacity = max(2, 2 * sub_rows // experts_all + 1)
    flat_routes = routes.reshape(-1)
    onehot_int = (flat_routes[:, None] == jnp.arange(experts_all, dtype=jnp.int32)[None, :]).astype(
        jnp.int32
    )
    earlier = jnp.cumsum(onehot_int, axis=0) - onehot_int
    rank_in = jnp.sum(earlier * onehot_int, axis=1)
    place_at = (
        flat_routes // local_experts * capacity * local_experts
        + rank_in * local_experts
        + flat_routes % local_experts
    )
    placement_plan = (
        place_at[:, None] == jnp.arange(experts_all * capacity, dtype=jnp.int32)[None, :]
    ).astype(jnp.bfloat16)
    paired_rows = jnp.repeat(normed_ffn, 2, axis=0)
    outgoing = jnp.einsum(
        "qe,qd->ed", placement_plan, paired_rows, preferred_element_type=jnp.float32
    )
    outgoing = outgoing.astype(jnp.bfloat16).reshape(n_req, capacity, local_experts, width)
    arrived = lax.all_to_all(outgoing, "req", split_axis=0, concat_axis=0, tiled=True)
    returned = lax.all_to_all(
        expert_apply(arrived, gate_up, down), "req", split_axis=0, concat_axis=0, tiled=True
    )
    back_rows = returned.reshape(experts_all * capacity, width)
    paired_output = jnp.dot(placement_plan, back_rows, preferred_element_type=jnp.float32).reshape(
        sub_rows, 2, width
    )
    mixed = residual.astype(jnp.float32) + jnp.sum(gates[:, :, None] * paired_output, axis=1)
    return mixed.astype(jnp.bfloat16)


def solution(mesh):
    in_specs = (
        P("req", "kv"),
        P(),
        P("req"),
        P("req", None),
        P("req", "kv", None, None),
        P(),
        P("kv", None, None),
        P("kv", None, None),
        P(),
        P(),
        P(("req", "kv"), None),
        P("req", None, None),
        P("req", None, None),
    )
    out_specs = P(("req", "kv"), None)
    return jax.shard_map(shards, mesh=mesh, in_specs=in_specs, out_specs=out_specs, check_vma=False)
```

profile of v0, /device:TPU:0, one launch (start us, length us, event | category | flops | bytes accessed | tf_op | source)
XLA Modules:
  0.0 223.6 jit_solution(11353303705725707446)
XLA Ops:
  6.5 2.1 fusion.66
  8.6 2.1 fusion.67
  10.7 2.1 fusion.68
  12.8 0.7 and_select_fusion
  13.4 1.6 fusion.69
  15.0 0.7 fusion.51
  15.8 0.1 reshape.339
  16.0 8.0 %scatter_custom_fusion = s32[320]{0:T(512)S(1)} fusion(s32[2048]{0:T(1024)S(1)} %bitcast.180, s32[2048]{0:T(1024)S(1)} %reshape.468, s32[]{:T(128)} %constant.102.clone.1), kind=kCustom, calls=%fused_computation.112 | custom fusion | bytes 1284 | tf_op jit(solution)/shard_map/scatter | solution.py:40
  24.1 0.6 broadcast_compare_fusion
  24.7 0.6 compare_select_fusion.2
  25.2 0.8 compare_and_fusion.1
  26.0 26.8 %all_gather.6 = bf16[1024,192]{1,0:T(8,128)(2,1)} all-gather(bf16[64,192]{1,0:T(8,128)(2,1)} %param.13), channel_id=1, replica_groups=mesh['req'=16,'kv'=8] {'req'}, dimensions={0}, use_global_device_ids=true | all-gather | bytes 417792 | tf_op jit(solution)/shard_map/all_gather | solution.py:123
  52.8 1.8 gather_fusion
  54.7 14.0 %all-gather = bf16[8,192,64]{1,2,0:T(8,128)(2,1)S(1)} all-gather(bf16[1,192,64]{1,2,0:T(8,128)(2,1)S(1)} %select_bitcast_fusion), channel_id=1, replica_groups=mesh['req'=16,'kv'=8] {'kv'}, dimensions={0}, use_global_device_ids=true | all-gather | bytes 221184 | tf_op jit(solution)/shard_map/all_gather | solution.py:126
  68.7 0.9 copy.104
  69.6 1.2 reshape.494
  70.8 0.1 fusion.21
  70.9 1.7 convolution_bitcast_fusion
  72.6 0.7 fusion.50
  73.3 8.2 %scatter_custom_fusion.1 = s32[320]{0:T(512)S(1)} fusion(s32[2048]{0:T(1024)S(1)} %bitcast.181, s32[2048]{0:T(1024)S(1)} %reshape.476, s32[]{:T(128)} %constant.106.clone.1), kind=kCustom, calls=%fused_computation.109 | custom fusion | bytes 1284 | tf_op jit(solution)/shard_map/scatter | solution.py:42
  81.6 0.6 broadcast_multiply_fusion
  82.2 0.1 copy.106
  82.3 0.1 copy.107
  82.4 0.7 pad_clamp_fusion
  83.1 2.5 %gather_fusion.1 = bf16[320,3,64]{2,1,0:T(4,128)(2,1)} fusion(bf16[64,3,64]{2,1,0:T(4,128)(2,1)S(1)} %copy.107, s32[1024]{0:T(1024)S(1)} %pad_clamp_fusion), kind=kCustom, calls=%fused_computation.1 | custom fusion | bytes 247040 | tf_op jit(solution)/shard_map/jit(_take)/gather | solution.py:47
  85.5 39.8 %select_select_fusion = s32[320]{0:T(512)S(1)} fusion(s32[]{:T(128)} %bitcast.5, s32[]{:T(128)} %bitcast.6, s32[]{:T(128)} %bitcast.7, s32[]{:T(128)} %bitcast.8, s32[]{:T(128)} %bitcast.9, s32[]{:T(128)} %bitcast.10, s32[]{:T(128)} %bitcast.11, s32[]{:T(128)} %bitcast.12, s32[]{:T(128)} %bitcast.13, s32[]{:T(128)} %bitcast.14, s32[]{:T(128)} %bitcast.15, ...), kind=kLoop, calls=%fused_computation.96 | loop fusion | flops 42880 | bytes 2816 | tf_op jit(solution)/shard_map/jit(_take)/select_n | solution.py:45
  125.4 0.9 fusion.36
  126.3 5.7 %fusion.70 = (f32[320,3]{1,0:T(8,128)}, f32[320,3,128]{2,1,0:T(4,128)}) fusion(bf16[320,1,128,128]{3,2,0,1:T(8,128)(2,1)} %bitcast.182, bf16[320,3,64]{2,1,0:T(4,128)(2,1)} %gather_fusion.1, pred[320]{0:T(512)(128)(4,1)} %get-tuple-element.16, pred[320,128]{1,0:T(8,128)(4,1)S(1)} %fusion.36), kind=kOutput, calls=%fused_computation.124 | convolution fusion | flops 16157760 | bytes 6107392 | tf_op jit(solution)/shard_map/pkgd,pkdt->pkgt/dot_general | solution.py:49
  131.9 1.0 copy.109
  132.9 0.9 fusion.48
  134.0 0.1 select_reduce_fusion
  134.1 0.1 copy.110
  134.2 1.6 gather_fusion.2
  135.8 1.0 broadcast_select_fusion
  136.9 1.9 fusion.19
  138.8 6.5 %fusion.2 = f32[320,3,64]{2,1,0:T(4,128)} fusion(bf16[320,1,128,128]{3,2,0,1:T(8,128)(2,1)} %bitcast.183, f32[320,3,128]{2,1,0:T(4,128)} %get-tuple-element.82, f32[320,3]{1,0:T(8,128)S(1)} %broadcast_select_fusion, pred[320,128]{1,0:T(8,128)(4,1)S(1)} %fusion.36), kind=kOutput, calls=%fused_computation.9 | convolution fusion | flops 16097280 | bytes 6188800 | tf_op jit(solution)/shard_map/pkgt,pkdt->pkgd/dot_general | solution.py:72
  145.2 0.2 convolution_add_fusion.1
  145.5 2.1 copy.112
  147.5 2.0 fusion.15
  149.5 0.9 copy.113
  150.4 2.0 convolution_convert_fusion
  152.4 0.1 copy.114
  152.5 0.1 eq.72
  152.7 0.2 select_reduce_fusion.1
  153.0 0.1 copy.117
  153.1 0.1 copy.118
  153.2 0.1 reshape.458
  153.3 28.5 %reduce-scatter.2.cloned.1.call-done = bf16[8,1536]{1,0:T(8,128)(2,1)} async-done(((bf16[64,1536]{1,0:T(8,128)(2,1)}), bf16[8,1536]{1,0:T(8,128)(2,1)}) %reduce-scatter.2.cloned.1.call-update) | async-done | bytes 24592 | tf_op jit(solution)/shard_map/reduce_scatter | solution.py:132
  181.9 0.9 fusion.41
  182.8 0.1 fusion.71
  182.9 0.7 gather_fusion.3
  183.7 0.3 convolution_convert_fusion.1
  184.0 0.7 reshape.351
  184.7 6.8 %all-to-all-start = ((bf16[16,2,1,1536]{3,1,2,0:T(2,128)(2,1)}), bf16[16,2,1,1536]{3,1,2,0:T(2,128)(2,1)S(1)}, u32[]{:S(2)}, u32[]{:S(2)}) async-start(bf16[16,2,1,1536]{3,1,2,0:T(2,128)(2,1)} %bitcast.90), calls=%async_computation.1 | async-start | bytes 196608 | tf_op jit(solution)/shard_map/all_to_all | solution.py:168
  191.5 0.1 divide_reduce_fusion
  191.7 7.7 %all-to-all-done = bf16[16,2,1,1536]{3,1,2,0:T(2,128)(2,1)S(1)} async-done(((bf16[16,2,1,1536]{3,1,2,0:T(2,128)(2,1)}), bf16[16,2,1,1536]{3,1,2,0:T(2,128)(2,1)S(1)}, u32[]{:S(2)}, u32[]{:S(2)}) %all-to-all-start) | async-done | bytes 98336 | tf_op jit(solution)/shard_map/all_to_all | solution.py:168
  199.4 4.0 %fusion.6 = f32[1,32,2048]{2,1,0:T(8,128)S(1)} fusion(bf16[32,1536]{1,0:T(8,128)(2,1)S(1)} %reshape.352, bf16[1,1536,2048]{2,1,0:T(8,128)(2,1)} %param.24), kind=kOutput, calls=%fused_computation.15 | convolution fusion | flops 201326592 | bytes 6651904 | tf_op jit(solution)/shard_map/erd,edf->erf/dot_general | solution.py:95
  203.4 0.6 fusion.9
  204.0 0.7 transpose_reshape.3
  204.6 3.5 %all-to-all-start.1 = ((bf16[16,2,1,1536]{3,1,2,0:T(2,128)(2,1)}), bf16[16,2,1,1536]{3,1,2,0:T(2,128)(2,1)S(1)}, u32[]{:S(2)}, u32[]{:S(2)}) async-start(bf16[16,2,1,1536]{3,1,2,0:T(2,128)(2,1)} %bitcast.95), calls=%async_computation.2 | async-start | bytes 196608 | tf_op jit(solution)/shard_map/all_to_all | solution.py:169
  208.2 0.1 copy.119
  208.3 7.6 %all-to-all-done.1 = bf16[16,2,1,1536]{3,1,2,0:T(2,128)(2,1)S(1)} async-done(((bf16[16,2,1,1536]{3,1,2,0:T(2,128)(2,1)}), bf16[16,2,1,1536]{3,1,2,0:T(2,128)(2,1)S(1)}, u32[]{:S(2)}, u32[]{:S(2)}) %all-to-all-start.1) | async-done | bytes 98336 | tf_op jit(solution)/shard_map/all_to_all | solution.py:169
  216.0 0.2 fusion.14
  216.2 0.6 fusion.44
  (39 shorter events, 1.2 us)
Async XLA Ops:
  6.5 196.8 %copy-start = (bf16[1,1024,1536]{2,1,0:T(8,128)(2,1)S(1)}, bf16[1,1024,1536]{2,1,0:T(8,128)(2,1)}, u32[]{:S(2)}) copy-start(bf16[1,1024,1536]{2,1,0:T(8,128)(2,1)} %param.25) | copy-start | bytes 9437188
  6.5 175.3 %reduce-scatter.2.cloned.1.call-start = ((), (), s32[]{:S(2)}) async-start(), calls=%async_computation.3 | async-start | bytes 221184 | tf_op jit(solution)/shard_map/reduce_scatter | solution.py:132
  134.2 18.2 %copy-start.3 = (s32[8,2]{0,1:T(2,128)S(1)}, s32[8,2]{0,1:T(2,128)}, u32[]{:S(2)}) copy-start(s32[8,2]{0,1:T(2,128)} %param.23) | copy-start | bytes 196
  134.2 48.5 %copy-start.2 = (f32[1536]{0:T(1024)S(1)}, f32[1536]{0:T(1024)}, u32[]{:S(2)}) copy-start(f32[1536]{0:T(1024)} %param.21) | copy-start | bytes 18436
  134.2 48.6 %copy-start.1 = (bf16[1536,16]{0,1:T(8,128)(2,1)S(1)}, bf16[1536,16]{0,1:T(8,128)(2,1)}, u32[]{:S(2)}) copy-start(bf16[1536,16]{0,1:T(8,128)(2,1)} %param.22) | copy-start | bytes 147460
  184.7 14.6 %all-to-all-start = ((bf16[16,2,1,1536]{3,1,2,0:T(2,128)(2,1)}), bf16[16,2,1,1536]{3,1,2,0:T(2,128)(2,1)S(1)}, u32[]{:S(2)}, u32[]{:S(2)}) async-start(bf16[16,2,1,1536]{3,1,2,0:T(2,128)(2,1)} %bitcast.90), calls=%async_computation.1 | async-start | bytes 196608 | tf_op jit(solution)/shard_map/all_to_all | solution.py:168
  204.6 11.3 %all-to-all-start.1 = ((bf16[16,2,1,1536]{3,1,2,0:T(2,128)(2,1)}), bf16[16,2,1,1536]{3,1,2,0:T(2,128)(2,1)S(1)}, u32[]{:S(2)}, u32[]{:S(2)}) async-start(bf16[16,2,1,1536]{3,1,2,0:T(2,128)(2,1)} %bitcast.95), calls=%async_computation.2 | async-start | bytes 196608 | tf_op jit(solution)/shard_map/all_to_all | solution.py:169
Sparse Core Ops, SparseCore 0:
  152.5 29.2 reduce-scatter.1
where the time goes:
time: 225 us; the launch traced here: 224 us
  other arithmetic  51.4 us (23%)
  waiting for transfers between devices  43.9 us (20%)
  blocking collectives  40.8 us (18%)
  local copies, waits for them, and re-layouts  39.5 us (18%)
  matrix products  24.1 us (11%)
  between operations  13.6 us (6%)
  starting transfers between devices  10.3 us (5%)
    select_n x2, other arithmetic, attend(): jnp.take(seq_lens, owner_safe)[:, None]  40.4 us
    reduce_scatter x1, waiting for transfers between devices, shards(): lax.psum_scatter(jnp.dot(head_out, out_flat, preferred_element_type=jnp.f...  28.5 us
    all_gather x1, blocking collectives, shards(): every_row = lax.all_gather(hidden, 'req', axis=0, tiled=True)  26.8 us
    all_gather x1, blocking collectives, shards(): tokens = lax.all_gather(picked_rows, 'kv', axis=1, tiled=True)  14 us
    scatter x1, local copies, waits for them, and re-layouts, attend(): jnp.zeros((pool_pages,), jnp.int32).at[target_page]  8.21 us
    scatter x1, local copies, waits for them, and re-layouts, attend(): jnp.full((pool_pages,), slot_count, jnp.int32).at[target_page]  8.03 us
    gather x4, local copies, waits for them, and re-layouts, attend(): jnp.take(seq_lens, owner_safe)[:, None]  7.79 us
    all_to_all x1, waiting for transfers between devices, shards(): lax.all_to_all(outgoing, 'req', split_axis=0, concat_axis=0, tiled=True)  7.69 us
  transfers between devices with their start and end apart: 3, of which 3 were waited for; matrix products, arithmetic and copies ran while one was open for 1% of the time, Pallas kernels for 0%

commit v1 on v0

--- a/solution.py
+++ b/solution.py
@@ -166,9 +166,19 @@
     )
     outgoing = outgoing.astype(jnp.bfloat16).reshape(n_req, capacity, local_experts, width)
     arrived = lax.all_to_all(outgoing, "req", split_axis=0, concat_axis=0, tiled=True)
-    returned = lax.all_to_all(
-        expert_apply(arrived, gate_up, down), "req", split_axis=0, concat_axis=0, tiled=True
-    )
+    value = expert_apply(arrived, gate_up, down)
+    ways, here = (lax.axis_size("req"), lax.axis_index("req"))
+    width_2 = value.shape[0] // ways
+    dims = list(value.shape)
+    dims[0] = width_2
+    height = dims[0]
+    dims[0] = height * ways
+    returned = jnp.zeros(dims, value.dtype)
+    for mask in range(ways):
+        part = lax.dynamic_slice_in_dim(value, (here ^ mask) * width_2, width_2, axis=0)
+        if mask:
+            part = lax.ppermute(part, "req", [(d, d ^ mask) for d in range(ways)])
+        returned = lax.dynamic_update_slice_in_dim(returned, part, (here ^ mask) * height, axis=0)
     back_rows = returned.reshape(experts_all * capacity, width)
     paired_output = jnp.dot(placement_plan, back_rows, preferred_element_type=jnp.float32).reshape(
         sub_rows, 2, width

time: 225 us -> 244 us (1.084)
  starting transfers between devices: 10.3 us -> 38.9 us
  waiting for transfers between devices: 43.9 us -> 38.6 us
  other arithmetic: 51.4 us -> 48.6 us
    ppermute x0 -> x15, starting transfers between devices: none -> 32.1 us  [shards(): part = lax.ppermute(part, 'req', [(d, d ^ mask) for d in range(ways)])]
    all_to_all x1 -> x0, waiting for transfers between devices: 7.62 us -> none  [shards(): lax.all_to_all(expert_apply(arrived, gate_up, down), 'req', split_axis=0,...]
    all_to_all x1 -> x0, starting transfers between devices: 3.51 us -> none  [shards(): lax.all_to_all(expert_apply(arrived, gate_up, down), 'req', split_axis=0,...]
    ppermute x0 -> x15, waiting for transfers between devices: none -> 3.17 us  [shards(): part = lax.ppermute(part, 'req', [(d, d ^ mask) for d in range(ways)])]
  transfers between devices with their start and end apart: 3 -> 17, of which waited for: 3 -> 3; matrix products, arithmetic and copies ran while one was open for 1% -> 1% of each run, Pallas kernels for 0% -> 0%
where the time goes in v1:
time: 244 us; the launch traced here: 243 us
  other arithmetic  48.6 us (20%)
  blocking collectives  40.8 us (17%)
  local copies, waits for them, and re-layouts  39.2 us (16%)
  starting transfers between devices  38.9 us (16%)
  waiting for transfers between devices  38.6 us (16%)
  matrix products  22.8 us (9%)
  between operations  13.9 us (6%)
    select_n x2, other arithmetic, attend(): jnp.take(seq_lens, owner_safe)[:, None]  40 us
    ppermute x15, starting transfers between devices, shards(): part = lax.ppermute(part, 'req', [(d, d ^ mask) for d in range(ways)])  32.1 us
    reduce_scatter x1, waiting for transfers between devices, shards(): lax.psum_scatter(jnp.dot(head_out, out_flat, preferred_element_type=jnp.f...  27.8 us
    all_gather x1, blocking collectives, shards(): every_row = lax.all_gather(hidden, 'req', axis=0, tiled=True)  26.8 us
    all_gather x1, blocking collectives, shards(): tokens = lax.all_gather(picked_rows, 'kv', axis=1, tiled=True)  14 us
    scatter x1, local copies, waits for them, and re-layouts, attend(): jnp.zeros((pool_pages,), jnp.int32).at[target_page]  8.21 us
    scatter x1, local copies, waits for them, and re-layouts, attend(): jnp.full((pool_pages,), slot_count, jnp.int32).at[target_page]  8.03 us
    gather x4, local copies, waits for them, and re-layouts, attend(): jnp.take(seq_lens, owner_safe)[:, None]  7.78 us
  transfers between devices with their start and end apart: 17, of which 3 were waited for; matrix products, arithmetic and copies ran while one was open for 1% of the time, Pallas kernels for 0%

profile of v1, /device:TPU:0, one launch (start us, length us, event | category | flops | bytes accessed | tf_op | source)
XLA Modules:
  0.0 243.0 jit_solution(4763796137871690094)
XLA Ops:
  6.5 2.1 fusion.66
  8.6 2.1 fusion.67
  10.7 2.1 fusion.68
  12.8 0.7 and_select_fusion
  13.4 1.6 fusion.69
  15.0 0.7 fusion.51
  16.0 8.0 %scatter_custom_fusion = s32[320]{0:T(512)S(1)} fusion(s32[2048]{0:T(1024)S(1)} %bitcast.179, s32[2048]{0:T(1024)S(1)} %reshape.468, s32[]{:T(128)} %constant.87.clone.1), kind=kCustom, calls=%fused_computation.144 | custom fusion | bytes 1284 | tf_op jit(solution)/shard_map/scatter | solution.py:40
  24.1 0.8 compare_and_fusion.1
  24.9 26.8 %all_gather.6 = bf16[1024,192]{1,0:T(8,128)(2,1)} all-gather(bf16[64,192]{1,0:T(8,128)(2,1)} %param.13), channel_id=1, replica_groups=mesh['req'=16,'kv'=8] {'req'}, dimensions={0}, use_global_device_ids=true | all-gather | bytes 417792 | tf_op jit(solution)/shard_map/all_gather | solution.py:123
  51.7 1.8 gather_fusion
  53.5 14.0 %all-gather = bf16[8,192,64]{1,2,0:T(8,128)(2,1)S(1)} all-gather(bf16[1,192,64]{1,2,0:T(8,128)(2,1)S(1)} %select_bitcast_fusion), channel_id=1, replica_groups=mesh['req'=16,'kv'=8] {'kv'}, dimensions={0}, use_global_device_ids=true | all-gather | bytes 221184 | tf_op jit(solution)/shard_map/all_gather | solution.py:126
  67.6 0.8 copy.102
  68.4 1.2 reshape.494
  69.6 0.1 fusion.21
  69.8 1.7 convolution_bitcast_fusion
  71.4 0.6 fusion.50
  72.1 8.2 %scatter_custom_fusion.1 = s32[320]{0:T(512)S(1)} fusion(s32[2048]{0:T(1024)S(1)} %bitcast.180, s32[2048]{0:T(1024)S(1)} %reshape.476, s32[]{:T(128)} %constant.88.clone.1), kind=kCustom, calls=%fused_computation.141 | custom fusion | bytes 1284 | tf_op jit(solution)/shard_map/scatter | solution.py:42
  80.6 2.5 %gather_fusion.1 = bf16[320,3,64]{2,1,0:T(4,128)(2,1)} fusion(bf16[64,3,64]{2,1,0:T(4,128)(2,1)S(1)} %copy.105, s32[1024]{0:T(1024)S(1)} %pad_clamp_fusion), kind=kCustom, calls=%fused_computation.1 | custom fusion | bytes 247040 | tf_op jit(solution)/shard_map/jit(_take)/gather | solution.py:47
  83.1 40.0 %select_select_fusion = s32[320]{0:T(512)S(1)} fusion(s32[]{:T(128)} %bitcast.5, s32[]{:T(128)} %bitcast.6, s32[]{:T(128)} %bitcast.7, s32[]{:T(128)} %bitcast.8, s32[]{:T(128)} %bitcast.9, s32[]{:T(128)} %bitcast.10, s32[]{:T(128)} %bitcast.11, s32[]{:T(128)} %bitcast.12, s32[]{:T(128)} %bitcast.13, s32[]{:T(128)} %bitcast.14, s32[]{:T(128)} %bitcast.15, ...), kind=kLoop, calls=%fused_computation.128 | loop fusion | flops 42880 | bytes 2816 | tf_op jit(solution)/shard_map/jit(_take)/select_n | solution.py:45
  123.0 0.2 fusion.36
  123.3 0.6 copy-done.1
  123.9 5.7 %fusion.70 = (f32[320,3]{1,0:T(8,128)}, f32[320,3,128]{2,1,0:T(4,128)}) fusion(bf16[320,1,128,128]{3,2,0,1:T(8,128)(2,1)} %bitcast.181, bf16[320,3,64]{2,1,0:T(4,128)(2,1)} %gather_fusion.1, pred[320]{0:T(512)(128)(4,1)S(1)} %get-tuple-element.32, pred[320,128]{1,0:T(8,128)(4,1)S(1)} %fusion.36), kind=kOutput, calls=%fused_computation.156 | convolution fusion | flops 16157760 | bytes 6107200 | tf_op jit(solution)/shard_map/pkgd,pkdt->pkgt/dot_general | solution.py:49
  129.5 1.0 copy.107
  130.5 0.2 fusion.48
  130.8 0.1 select_reduce_fusion
  131.0 0.6 convert_bitcast_fusion
  131.7 1.1 gather_fusion.2
  132.8 0.7 broadcast_select_fusion
  133.5 1.9 fusion.19
  135.4 6.5 %fusion.2 = f32[320,3,64]{2,1,0:T(4,128)} fusion(bf16[320,1,128,128]{3,2,0,1:T(8,128)(2,1)} %bitcast.182, f32[320,3,128]{2,1,0:T(4,128)} %get-tuple-element.98, f32[320,3]{1,0:T(8,128)S(1)} %broadcast_select_fusion, pred[320,128]{1,0:T(8,128)(4,1)} %copy-done.1), kind=kOutput, calls=%fused_computation.9 | convolution fusion | flops 16097280 | bytes 6188800 | tf_op jit(solution)/shard_map/pkgt,pkdt->pkgd/dot_general | solution.py:72
  141.9 0.2 convolution_add_fusion.1
  142.1 2.1 copy.110
  144.2 1.3 fusion.15
  145.7 2.0 convolution_convert_fusion
  147.7 0.8 copy.112
  148.7 0.2 select_reduce_fusion.1
  149.4 27.8 %reduce-scatter.2.cloned.1.call-done = bf16[8,1536]{1,0:T(8,128)(2,1)} async-done(((bf16[64,1536]{1,0:T(8,128)(2,1)}), bf16[8,1536]{1,0:T(8,128)(2,1)}) %reduce-scatter.2.cloned.1.call-update) | async-done | bytes 24592 | tf_op jit(solution)/shard_map/reduce_scatter | solution.py:132
  177.1 0.9 fusion.41
  178.1 0.1 fusion.71
  178.2 0.7 gather_fusion.3
  179.0 0.3 convolution_convert_fusion.1
  179.3 0.7 reshape.351
  180.0 6.8 %all-to-all-start = ((bf16[16,2,1,1536]{3,1,2,0:T(2,128)(2,1)}), bf16[16,2,1,1536]{3,1,2,0:T(2,128)(2,1)S(1)}, u32[]{:S(2)}, u32[]{:S(2)}) async-start(bf16[16,2,1,1536]{3,1,2,0:T(2,128)(2,1)} %bitcast.90), calls=%async_computation.1 | async-start | bytes 196608 | tf_op jit(solution)/shard_map/all_to_all | solution.py:168
  186.9 7.7 %all-to-all-done = bf16[16,2,1,1536]{3,1,2,0:T(2,128)(2,1)S(1)} async-done(((bf16[16,2,1,1536]{3,1,2,0:T(2,128)(2,1)}), bf16[16,2,1,1536]{3,1,2,0:T(2,128)(2,1)S(1)}, u32[]{:S(2)}, u32[]{:S(2)}) %all-to-all-start) | async-done | bytes 98336 | tf_op jit(solution)/shard_map/all_to_all | solution.py:168
  194.6 4.0 %fusion.6 = f32[1,32,2048]{2,1,0:T(8,128)S(1)} fusion(bf16[32,1536]{1,0:T(8,128)(2,1)S(1)} %reshape.352, bf16[1,1536,2048]{2,1,0:T(8,128)(2,1)} %param.24), kind=kOutput, calls=%fused_computation.15 | convolution fusion | flops 201326592 | bytes 6651904 | tf_op jit(solution)/shard_map/erd,edf->erf/dot_general | solution.py:95
  198.6 0.6 fusion.9
  199.4 0.1 constant_dynamic-slice_fusion
  199.5 0.6 collective-permute-start
  200.3 2.0 collective-permute-start.1
  202.3 2.2 collective-permute-start.2
  204.4 0.4 collective-permute-start.3
  204.8 0.4 collective-permute-start.4
  205.3 3.2 %collective-permute-start.5 = (bf16[1,2,1,1536]{3,1,0,2:T(2,128)(2,1)S(1)}, bf16[1,2,1,1536]{3,1,0,2:T(2,128)(2,1)S(1)}, u32[]{:S(2)}, u32[]{:S(2)}) collective-permute-start(bf16[1,2,1,1536]{3,1,0,2:T(2,128)(2,1)S(1)} %get-tuple-element.18), channel_id=1, source_target_pairs={{0,48},{8,56},{16,32},{24,40},{32,16},{40,24},{48,0},{56,8},{64,11... | collective-permute-start | bytes 18440 | tf_op jit(solution)/shard_map/ppermute | solution.py:180
  208.5 3.1 %collective-permute-start.6 = (bf16[1,2,1,1536]{3,1,0,2:T(2,128)(2,1)S(1)}, bf16[1,2,1,1536]{3,1,0,2:T(2,128)(2,1)S(1)}, u32[]{:S(2)}, u32[]{:S(2)}) collective-permute-start(bf16[1,2,1,1536]{3,1,0,2:T(2,128)(2,1)S(1)} %get-tuple-element.17), channel_id=1, source_target_pairs={{0,56},{8,48},{16,40},{24,32},{32,24},{40,16},{48,8},{56,0},{64,12... | collective-permute-start | bytes 18440 | tf_op jit(solution)/shard_map/ppermute | solution.py:180
  211.6 1.1 collective-permute-start.7
  212.8 0.1 collective-permute-start.8
  213.0 5.1 %collective-permute-start.9 = (bf16[1,2,1,1536]{3,1,0,2:T(2,128)(2,1)S(1)}, bf16[1,2,1,1536]{3,1,0,2:T(2,128)(2,1)S(1)}, u32[]{:S(2)}, u32[]{:S(2)}) collective-permute-start(bf16[1,2,1,1536]{3,1,0,2:T(2,128)(2,1)S(1)} %get-tuple-element.14), channel_id=1, source_target_pairs={{0,80},{8,88},{16,64},{24,72},{32,112},{40,120},{48,96},{56,104},{... | collective-permute-start | bytes 18440 | tf_op jit(solution)/shard_map/ppermute | solution.py:180
  218.1 4.0 %collective-permute-start.10 = (bf16[1,2,1,1536]{3,1,0,2:T(2,128)(2,1)S(1)}, bf16[1,2,1,1536]{3,1,0,2:T(2,128)(2,1)S(1)}, u32[]{:S(2)}, u32[]{:S(2)}) collective-permute-start(bf16[1,2,1,1536]{3,1,0,2:T(2,128)(2,1)S(1)} %get-tuple-element.13), channel_id=1, source_target_pairs={{0,88},{8,80},{16,72},{24,64},{32,120},{40,112},{48,104},{56,96},{... | collective-permute-start | bytes 18440 | tf_op jit(solution)/shard_map/ppermute | solution.py:180
  222.1 1.1 collective-permute-start.11
  223.3 4.9 %collective-permute-start.13 = (bf16[1,2,1,1536]{3,1,0,2:T(2,128)(2,1)S(1)}, bf16[1,2,1,1536]{3,1,0,2:T(2,128)(2,1)S(1)}, u32[]{:S(2)}, u32[]{:S(2)}) collective-permute-start(bf16[1,2,1,1536]{3,1,0,2:T(2,128)(2,1)S(1)} %get-tuple-element.10), channel_id=1, source_target_pairs={{0,112},{8,120},{16,96},{24,104},{32,80},{40,88},{48,64},{56,72},{... | collective-permute-start | bytes 18440 | tf_op jit(solution)/shard_map/ppermute | solution.py:180
  228.2 3.8 %collective-permute-start.14 = (bf16[1,2,1,1536]{3,1,0,2:T(2,128)(2,1)S(1)}, bf16[1,2,1,1536]{3,1,0,2:T(2,128)(2,1)S(1)}, u32[]{:S(2)}, u32[]{:S(2)}) collective-permute-start(bf16[1,2,1,1536]{3,1,0,2:T(2,128)(2,1)S(1)} %get-tuple-element.9), channel_id=1, source_target_pairs={{0,120},{8,112},{16,104},{24,96},{32,88},{40,80},{48,72},{56,64},{... | collective-permute-start | bytes 18440 | tf_op jit(solution)/shard_map/ppermute | solution.py:180
  232.1 3.1 %collective-permute-done.14 = bf16[1,2,1,1536]{3,1,0,2:T(2,128)(2,1)S(1)} collective-permute-done((bf16[1,2,1,1536]{3,1,0,2:T(2,128)(2,1)S(1)}, bf16[1,2,1,1536]{3,1,0,2:T(2,128)(2,1)S(1)}, u32[]{:S(2)}, u32[]{:S(2)}) %collective-permute-start.14) | collective-permute-done | bytes 6176 | tf_op jit(solution)/shard_map/ppermute | solution.py:180
  235.3 0.2 fusion.14
  235.5 0.6 fusion.44
  (90 shorter events, 2.7 us)
Async XLA Ops:
  6.5 192.1 %copy-start = (bf16[1,1024,1536]{2,1,0:T(8,128)(2,1)S(1)}, bf16[1,1024,1536]{2,1,0:T(8,128)(2,1)}, u32[]{:S(2)}) copy-start(bf16[1,1024,1536]{2,1,0:T(8,128)(2,1)} %param.25) | copy-start | bytes 9437188
  6.5 170.6 %reduce-scatter.2.cloned.1.call-start = ((), (), s32[]{:S(2)}) async-start(), calls=%async_computation.2 | async-start | bytes 221184 | tf_op jit(solution)/shard_map/reduce_scatter | solution.py:132
  24.1 106.5 %copy-start.6 = (pred[320]{0:T(512)(128)(4,1)}, pred[320]{0:T(512)(128)(4,1)S(1)}, u32[]{:S(2)}) copy-start(pred[320]{0:T(512)(128)(4,1)S(1)} %get-tuple-element.32) | copy-start | bytes 964
  123.2 0.6 copy-start.1
  132.7 11.5 %copy-start.5 = (bf16[64,1,3]{0,2,1:T(4,128)(2,1)S(1)}, bf16[64,1,3]{0,2,1:T(4,128)(2,1)}, u32[]{:S(2)}) copy-start(bf16[64,1,3]{0,2,1:T(4,128)(2,1)} %get-tuple-element.29) | copy-start | bytes 1156
  132.7 11.5 %copy-start.3 = (f32[64,64]{1,0:T(8,128)S(1)}, f32[64,64]{1,0:T(8,128)}, u32[]{:S(2)}) copy-start(f32[64,64]{1,0:T(8,128)} %get-tuple-element.25) | copy-start | bytes 49156
  133.5 44.5 %copy-start.4 = (f32[1536]{0:T(1024)S(1)}, f32[1536]{0:T(1024)}, u32[]{:S(2)}) copy-start(f32[1536]{0:T(1024)} %param.21) | copy-start | bytes 18436
  133.5 44.6 %copy-start.2 = (bf16[1536,16]{0,1:T(8,128)(2,1)S(1)}, bf16[1536,16]{0,1:T(8,128)(2,1)}, u32[]{:S(2)}) copy-start(bf16[1536,16]{0,1:T(8,128)(2,1)} %param.22) | copy-start | bytes 147460
  180.0 14.6 %all-to-all-start = ((bf16[16,2,1,1536]{3,1,2,0:T(2,128)(2,1)}), bf16[16,2,1,1536]{3,1,2,0:T(2,128)(2,1)S(1)}, u32[]{:S(2)}, u32[]{:S(2)}) async-start(bf16[16,2,1,1536]{3,1,2,0:T(2,128)(2,1)} %bitcast.90), calls=%async_computation.1 | async-start | bytes 196608 | tf_op jit(solution)/shard_map/all_to_all | solution.py:168
  199.5 5.8 %collective-permute-start = (bf16[1,2,1,1536]{3,1,0,2:T(2,128)(2,1)S(1)}, bf16[1,2,1,1536]{3,1,0,2:T(2,128)(2,1)S(1)}, u32[]{:S(2)}, u32[]{:S(2)}) collective-permute-start(bf16[1,2,1,1536]{3,1,0,2:T(2,128)(2,1)S(1)} %get-tuple-element.23), channel_id=1, source_target_pairs={{0,8},{8,0},{16,24},{24,16},{32,40},{40,32},{48,56},{56,48},{64,72... | collective-permute-start | bytes 18440 | tf_op jit(solution)/shard_map/ppermute | solution.py:180
  200.3 8.2 %collective-permute-start.1 = (bf16[1,2,1,1536]{3,1,0,2:T(2,128)(2,1)S(1)}, bf16[1,2,1,1536]{3,1,0,2:T(2,128)(2,1)S(1)}, u32[]{:S(2)}, u32[]{:S(2)}) collective-permute-start(bf16[1,2,1,1536]{3,1,0,2:T(2,128)(2,1)S(1)} %get-tuple-element.22), channel_id=1, source_target_pairs={{0,16},{8,24},{16,0},{24,8},{32,48},{40,56},{48,32},{56,40},{64,80... | collective-permute-start | bytes 18440 | tf_op jit(solution)/shard_map/ppermute | solution.py:180
  202.3 9.4 %collective-permute-start.2 = (bf16[1,2,1,1536]{3,1,0,2:T(2,128)(2,1)S(1)}, bf16[1,2,1,1536]{3,1,0,2:T(2,128)(2,1)S(1)}, u32[]{:S(2)}, u32[]{:S(2)}) collective-permute-start(bf16[1,2,1,1536]{3,1,0,2:T(2,128)(2,1)S(1)} %get-tuple-element.21), channel_id=1, source_target_pairs={{0,24},{8,16},{16,8},{24,0},{32,56},{40,48},{48,40},{56,32},{64,88... | collective-permute-start | bytes 18440 | tf_op jit(solution)/shard_map/ppermute | solution.py:180
  204.4 8.4 %collective-permute-start.3 = (bf16[1,2,1,1536]{3,1,0,2:T(2,128)(2,1)S(1)}, bf16[1,2,1,1536]{3,1,0,2:T(2,128)(2,1)S(1)}, u32[]{:S(2)}, u32[]{:S(2)}) collective-permute-start(bf16[1,2,1,1536]{3,1,0,2:T(2,128)(2,1)S(1)} %get-tuple-element.20), channel_id=1, source_target_pairs={{0,32},{8,40},{16,48},{24,56},{32,0},{40,8},{48,16},{56,24},{64,96... | collective-permute-start | bytes 18440 | tf_op jit(solution)/shard_map/ppermute | solution.py:180
  204.8 8.1 %collective-permute-start.4 = (bf16[1,2,1,1536]{3,1,0,2:T(2,128)(2,1)S(1)}, bf16[1,2,1,1536]{3,1,0,2:T(2,128)(2,1)S(1)}, u32[]{:S(2)}, u32[]{:S(2)}) collective-permute-start(bf16[1,2,1,1536]{3,1,0,2:T(2,128)(2,1)S(1)} %get-tuple-element.19), channel_id=1, source_target_pairs={{0,40},{8,32},{16,56},{24,48},{32,8},{40,0},{48,24},{56,16},{64,10... | collective-permute-start | bytes 18440 | tf_op jit(solution)/shard_map/ppermute | solution.py:180
  205.3 12.8 %collective-permute-start.5 = (bf16[1,2,1,1536]{3,1,0,2:T(2,128)(2,1)S(1)}, bf16[1,2,1,1536]{3,1,0,2:T(2,128)(2,1)S(1)}, u32[]{:S(2)}, u32[]{:S(2)}) collective-permute-start(bf16[1,2,1,1536]{3,1,0,2:T(2,128)(2,1)S(1)} %get-tuple-element.18), channel_id=1, source_target_pairs={{0,48},{8,56},{16,32},{24,40},{32,16},{40,24},{48,0},{56,8},{64,11... | collective-permute-start | bytes 18440 | tf_op jit(solution)/shard_map/ppermute | solution.py:180
  208.5 13.6 %collective-permute-start.6 = (bf16[1,2,1,1536]{3,1,0,2:T(2,128)(2,1)S(1)}, bf16[1,2,1,1536]{3,1,0,2:T(2,128)(2,1)S(1)}, u32[]{:S(2)}, u32[]{:S(2)}) collective-permute-start(bf16[1,2,1,1536]{3,1,0,2:T(2,128)(2,1)S(1)} %get-tuple-element.17), channel_id=1, source_target_pairs={{0,56},{8,48},{16,40},{24,32},{32,24},{40,16},{48,8},{56,0},{64,12... | collective-permute-start | bytes 18440 | tf_op jit(solution)/shard_map/ppermute | solution.py:180
  211.6 11.6 %collective-permute-start.7 = (bf16[1,2,1,1536]{3,1,0,2:T(2,128)(2,1)S(1)}, bf16[1,2,1,1536]{3,1,0,2:T(2,128)(2,1)S(1)}, u32[]{:S(2)}, u32[]{:S(2)}) collective-permute-start(bf16[1,2,1,1536]{3,1,0,2:T(2,128)(2,1)S(1)} %get-tuple-element.16), channel_id=1, source_target_pairs={{0,64},{8,72},{16,80},{24,88},{32,96},{40,104},{48,112},{56,120},{... | collective-permute-start | bytes 18440 | tf_op jit(solution)/shard_map/ppermute | solution.py:180
  212.8 10.5 %collective-permute-start.8 = (bf16[1,2,1,1536]{3,1,0,2:T(2,128)(2,1)S(1)}, bf16[1,2,1,1536]{3,1,0,2:T(2,128)(2,1)S(1)}, u32[]{:S(2)}, u32[]{:S(2)}) collective-permute-start(bf16[1,2,1,1536]{3,1,0,2:T(2,128)(2,1)S(1)} %get-tuple-element.15), channel_id=1, source_target_pairs={{0,72},{8,64},{16,88},{24,80},{32,104},{40,96},{48,120},{56,112},{... | collective-permute-start | bytes 18440 | tf_op jit(solution)/shard_map/ppermute | solution.py:180
  213.0 15.3 %collective-permute-start.9 = (bf16[1,2,1,1536]{3,1,0,2:T(2,128)(2,1)S(1)}, bf16[1,2,1,1536]{3,1,0,2:T(2,128)(2,1)S(1)}, u32[]{:S(2)}, u32[]{:S(2)}) collective-permute-start(bf16[1,2,1,1536]{3,1,0,2:T(2,128)(2,1)S(1)} %get-tuple-element.14), channel_id=1, source_target_pairs={{0,80},{8,88},{16,64},{24,72},{32,112},{40,120},{48,96},{56,104},{... | collective-permute-start | bytes 18440 | tf_op jit(solution)/shard_map/ppermute | solution.py:180
  218.1 13.9 %collective-permute-start.10 = (bf16[1,2,1,1536]{3,1,0,2:T(2,128)(2,1)S(1)}, bf16[1,2,1,1536]{3,1,0,2:T(2,128)(2,1)S(1)}, u32[]{:S(2)}, u32[]{:S(2)}) collective-permute-start(bf16[1,2,1,1536]{3,1,0,2:T(2,128)(2,1)S(1)} %get-tuple-element.13), channel_id=1, source_target_pairs={{0,88},{8,80},{16,72},{24,64},{32,120},{40,112},{48,104},{56,96},{... | collective-permute-start | bytes 18440 | tf_op jit(solution)/shard_map/ppermute | solution.py:180
  222.1 9.9 %collective-permute-start.11 = (bf16[1,2,1,1536]{3,1,0,2:T(2,128)(2,1)S(1)}, bf16[1,2,1,1536]{3,1,0,2:T(2,128)(2,1)S(1)}, u32[]{:S(2)}, u32[]{:S(2)}) collective-permute-start(bf16[1,2,1,1536]{3,1,0,2:T(2,128)(2,1)S(1)} %get-tuple-element.12), channel_id=1, source_target_pairs={{0,96},{8,104},{16,112},{24,120},{32,64},{40,72},{48,80},{56,88},{... | collective-permute-start | bytes 18440 | tf_op jit(solution)/shard_map/ppermute | solution.py:180
  223.2 8.8 %collective-permute-start.12 = (bf16[1,2,1,1536]{3,1,0,2:T(2,128)(2,1)S(1)}, bf16[1,2,1,1536]{3,1,0,2:T(2,128)(2,1)S(1)}, u32[]{:S(2)}, u32[]{:S(2)}) collective-permute-start(bf16[1,2,1,1536]{3,1,0,2:T(2,128)(2,1)S(1)} %get-tuple-element.11), channel_id=1, source_target_pairs={{0,104},{8,96},{16,120},{24,112},{32,72},{40,64},{48,88},{56,80},{... | collective-permute-start | bytes 18440 | tf_op jit(solution)/shard_map/ppermute | solution.py:180
  223.3 8.8 %collective-permute-start.13 = (bf16[1,2,1,1536]{3,1,0,2:T(2,128)(2,1)S(1)}, bf16[1,2,1,1536]{3,1,0,2:T(2,128)(2,1)S(1)}, u32[]{:S(2)}, u32[]{:S(2)}) collective-permute-start(bf16[1,2,1,1536]{3,1,0,2:T(2,128)(2,1)S(1)} %get-tuple-element.10), channel_id=1, source_target_pairs={{0,112},{8,120},{16,96},{24,104},{32,80},{40,88},{48,64},{56,72},{... | collective-permute-start | bytes 18440 | tf_op jit(solution)/shard_map/ppermute | solution.py:180
  228.2 7.0 %collective-permute-start.14 = (bf16[1,2,1,1536]{3,1,0,2:T(2,128)(2,1)S(1)}, bf16[1,2,1,1536]{3,1,0,2:T(2,128)(2,1)S(1)}, u32[]{:S(2)}, u32[]{:S(2)}) collective-permute-start(bf16[1,2,1,1536]{3,1,0,2:T(2,128)(2,1)S(1)} %get-tuple-element.9), channel_id=1, source_target_pairs={{0,120},{8,112},{16,104},{24,96},{32,88},{40,80},{48,72},{56,64},{... | collective-permute-start | bytes 18440 | tf_op jit(solution)/shard_map/ppermute | solution.py:180
Sparse Core Ops, SparseCore 0:
  147.8 29.2 reduce-scatter.1
